TPU v7x, 128 devices: a whole 4x4x4 slice. The times are simulated.
128 devices in a mesh: gz: 64 (over x, y_lo, z, core), xy: 2 (over y_hi).
Axes of the slice: x: 4, y: 4 (y_hi: 2, y_lo: 2; y = y_hi * 2 + y_lo), z: 4, core: 2. Of those that a mesh axis runs over, the one named last changes fastest.
Arguments:
- moments: bfloat16 [361, 512, 256], P(None, 'gz', 'xy'), may hold values from -4 to 4
- counts: int32 [512, 256], P('gz', 'xy'), may hold values from 0 to 7
- m2x: bfloat16 [1296, 361], replicated, may hold values from -0.3125 to 0.3125
- x2l: bfloat16 [361, 1296], replicated, may hold values from -0.0625 to 0.0625
- decay_rate: float32 [648], replicated, may hold values from 0.00048828125 to 0.05
- wave_x: float32 [648], replicated, may hold values from -3.140625 to 3.140625
- wave_y: float32 [648], replicated, may hold values from -3.140625 to 3.140625
- offsets: int32 [6, 2], replicated, may hold values from -2 to 2, as said below
Outputs:
- local_out: bfloat16 [361, 512, 256], P(None, 'gz', 'xy')
Inputs may be any that keep to these rules, and one draw needn't show every extreme that they name: `offsets`: some row is (2, -2) and some row is (-2, 2).
All inputs are finite; a program needn't handle non-finite values.
Results may differ from a plain program's by a relative error of at most 0.0064.
Values may be sent and summed in bfloat16 or wider, within the bound.
No kernel may reach another device: no remote copies, remote signals or barrier semaphores. Data moves between devices by JAX's collectives and lax.ppermute only.
A program may use at most 192 MiB of HBM per device.

v0:
```python
import jax
import jax.numpy as jnp
from jax import lax
from jax.sharding import PartitionSpec as P

BY = 8
R = 2
NOFF = 6


def from_behind(value, axis, steps):
    count = lax.axis_size(axis)
    pairs = [(source, (source + steps) % count) for source in range(count)]
    return lax.ppermute(value, axis, pairs)


def entering_2(part, axis, combine, identity):
    place = lax.axis_index(axis)
    gathered = jax.tree.map(lambda a: lax.all_gather(a, axis), part)
    state = jax.tree.map(lambda a, e: jnp.zeros_like(a) + jnp.asarray(e, a.dtype), part, identity)

    def one(turn, state):
        return combine(
            state, jax.tree.map(lambda a: lax.dynamic_index_in_dim(a, turn, 0, False), gathered)
        )

    return lax.fori_loop(0, place, one, state)


def extended(block, sides, width):
    for axis, dim in sides:
        count = lax.axis_size(axis)
        forward = [(i, i + 1) for i in range(count - 1)]
        forward.append((count - 1, 0))
        backward = [(target, source) for source, target in forward]
        low = lax.ppermute(
            lax.slice_in_dim(block, block.shape[dim] - width, None, axis=dim), axis, forward
        )
        high = lax.ppermute(lax.slice_in_dim(block, 0, width, axis=dim), axis, backward)
        block = jnp.concatenate([low, block, high], axis=dim)
    return block


def build_upward(box_terms, entering, before_term, rate_col, factor):
    layers = box_terms.shape[1]
    layer_pos = jnp.arange(layers, dtype=jnp.float32)
    layer_gap = layer_pos[:, None] - layer_pos[None, :]
    decay_table = jnp.where(
        layer_gap[None] >= 2.0,
        jnp.exp(-rate_col[:, :, None] * jnp.maximum(layer_gap, 0.0)[None]),
        0.0,
    )
    upward = jnp.einsum("kij,kjb->kib", decay_table, box_terms, precision=lax.Precision.HIGHEST)
    upward = (
        upward + jnp.exp(-rate_col * (layer_pos + 1.0)[None, :])[:, :, None] * entering[:, None, :]
    )
    upward = upward.at[:, 0, :].add(-factor * before_term)
    return upward


def body(moments, counts, m2x, x2l, decay_rate, wave_x, wave_y, offsets):
    coeffs, layers, plane_size = moments.shape
    exp_rows = m2x.shape[0]
    half_rows = exp_rows // 2
    columns = plane_size // BY
    loop_size = lax.axis_size("gz")
    slab_pos = lax.axis_index("gz").astype(jnp.float32)
    rate_col = jnp.concatenate([decay_rate, decay_rate])[:, None]
    factor = jnp.exp(-rate_col)
    weight = jnp.sqrt(1.0 - factor * factor)
    multipole = (moments.astype(jnp.float32) * counts.astype(jnp.float32)[None]).astype(
        jnp.bfloat16
    )
    expansion = jnp.dot(
        m2x, multipole.reshape(coeffs, layers * plane_size), preferred_element_type=jnp.float32
    )
    box_terms = (weight * expansion).reshape(exp_rows, layers, plane_size)
    layer_pos = jnp.arange(layers, dtype=jnp.float32)
    tail_power = jnp.exp(-rate_col * (layers - 1.0 - layer_pos)[None, :])
    outgoing = jnp.einsum("kz,kzb->kb", tail_power, box_terms, precision=lax.Precision.HIGHEST)
    before_term = from_behind(box_terms[:, layers - 1, :].astype(jnp.bfloat16), "gz", 1).astype(
        jnp.float32
    )
    slab_decay = jnp.exp(-rate_col * layers)
    lap_gain = 1.0 - jnp.exp(-rate_col * (layers * loop_size))

    def combine(earlier, later):
        return (earlier[0] * later[0], later[0] * earlier[1] + later[1])

    identity = (jnp.ones_like(slab_decay), jnp.zeros_like(outgoing))
    _, prefix = entering_2((slab_decay, outgoing), "gz", combine, identity)
    scaled = jnp.exp(-rate_col * (layers * (loop_size - 1.0 - slab_pos))) * outgoing
    lap_sum = lax.psum(scaled, "gz")
    entering = prefix + jnp.exp(-rate_col * (layers * slab_pos)) * lap_sum / lap_gain
    upward = build_upward(box_terms, entering, before_term, rate_col, factor)
    field_grid = upward.astype(jnp.bfloat16).reshape(exp_rows, layers, columns, BY)
    padded = extended(field_grid, (("xy", 2),), R)
    acc_real = jnp.zeros((half_rows, layers, columns, BY), jnp.float32)
    acc_imag = jnp.zeros((half_rows, layers, columns, BY), jnp.float32)
    for list_entry in range(NOFF):
        step_x = offsets[list_entry, 0]
        step_y = offsets[list_entry, 1]
        moved = lax.dynamic_slice_in_dim(padded, R - step_x, columns, 2)
        moved = jnp.roll(moved, step_y, axis=3)
        phase_angle = wave_x * step_x.astype(jnp.float32) + wave_y * step_y.astype(jnp.float32)
        cosine = jnp.cos(phase_angle)[:, None, None, None]
        sine_part = jnp.sin(phase_angle)[:, None, None, None]
        part_real = moved[:half_rows].astype(jnp.float32)
        part_imag = moved[half_rows:].astype(jnp.float32)
        acc_real = acc_real + part_real * cosine - part_imag * sine_part
        acc_imag = acc_imag + part_real * sine_part + part_imag * cosine
    shifted = (
        jnp.concatenate([acc_real, acc_imag], axis=0)
        .astype(jnp.bfloat16)
        .reshape(exp_rows, layers * plane_size)
    )
    local_out = jnp.dot(x2l, shifted, preferred_element_type=jnp.float32).astype(jnp.bfloat16)
    return local_out.reshape(coeffs, layers, plane_size)


def solution(mesh):
    in_specs = (P(None, "gz", "xy"), P("gz", "xy"), P(), P(), P(), P(), P(), P())
    out_specs = P(None, "gz", "xy")
    return jax.shard_map(body, mesh=mesh, in_specs=in_specs, out_specs=out_specs, check_vma=False)
```

profile of v0, /device:TPU:0, one launch (start us, length us, event | category | flops | bytes accessed | tf_op | source)
XLA Modules:
  0.0 901.1 jit_solution(17682668748722414921)
XLA Ops:
  10.6 1.6 multiply_bitcast_fusion
  13.5 9.6 %fusion.68 = f32[1296,1,128]{2,1,0:T(1,128)} fusion(f32[1296,8,1]{1,2,0:T(1,128)S(1)} %copy.17, f32[1296,8,128]{2,1,0:T(8,128)S(1)} %bitcast.59), kind=kOutput, calls=%fused_computation.135 | convolution fusion | flops 15925248 | bytes 6013440 | tf_op jit(solution)/shard_map/kz,kzb->kb/dot_general | solution.py:80
  23.1 2.9 slice.133
  27.7 85.2 %all_gather.10 = f32[64,1296,1]{1,2,0:T(1,128)S(1)} all-gather(f32[1,1296,1]{1,2,0:T(1,128)S(1)} %fusion.49), channel_id=1, replica_groups=mesh['gz'=64,'xy'=2] {'gz'}, dimensions={0}, use_global_device_ids=true | all-gather | bytes 336960 | tf_op jit(solution)/shard_map/all_gather | solution.py:19
  113.2 147.7 %all-gather.3.cloned.1.call-done = f32[82944,128]{1,0:T(8,128)} async-done(((f32[1296,128]{1,0:T(8,128)}), f32[82944,128]{1,0:T(8,128)}) %all-gather.3.cloned.1.call-update) | async-done | bytes 42467344 | tf_op jit(solution)/shard_map/all_gather | solution.py:19
  261.2 518.6 %all-reduce.2.cloned.1.call-done = f32[1296,128]{1,0:T(8,128)} async-done(((f32[1296,128]{1,0:T(8,128)}), f32[1296,128]{1,0:T(8,128)}) %all-reduce.2.cloned.1.call-update) | async-done | bytes 663568 | tf_op jit(solution)/shard_map/psum | solution.py:93
  779.7 1.5 divide_add_fusion
  781.2 13.8 %multiply_add_fusion = f32[1296,8,128]{2,1,0:T(8,128)S(1)} fusion(f32[1296,128]{1,0:T(8,128)S(1)} %divide_add_fusion, f32[1296,8]{1,0:T(8,128)S(1)} %copy.14, f32[1296,8,128]{2,1,0:T(8,128)} %bitcast.61, f32[8,8]{1,0:T(8,128)S(1)} %fusion.50, f32[1296]{0:T(1024)S(1)} %get-tuple-element.100, pred[8,8]{1,0:T(8,128)(4,1)S(1)} %fusion.51), kind=kOutput, calls=%fused_computation.14 | convolution fusion | flops 130222080 | bytes 11327360 | tf_op jit(solution)/shard_map/kij,kjb->kib/dot_general | solution.py:53
  795.1 2.4 copy-done.3
  798.2 18.9 %scatter-add.4 = f32[1296,8,128]{2,1,0:T(8,128)} dynamic-update-slice(f32[1296,8,128]{2,1,0:T(8,128)} %copy-done.3, f32[1296,1,128]{2,1,0:T(1,128)S(1)} %slice_add_fusion, s32[]{:T(128)} %constant.97.clone.1, s32[]{:T(128)} %constant.97.clone.1, s32[]{:T(128)} %constant.97.clone.1) | dynamic-update-slice | bytes 1327108 | tf_op jit(solution)/shard_map/scatter-add | solution.py:57
  817.1 3.8 convert_element_type.126
  820.8 4.9 copy.16
  826.9 3.2 collective-permute-start.1
  856.9 2.1 pad_maximum_fusion
  859.0 3.4 constant_dynamic-slice_fusion.5
  862.4 4.7 fusion.29
  867.1 2.0 fusion.30
  869.1 2.0 fusion.31
  871.2 2.1 fusion.32
  873.3 2.1 fusion.33
  875.3 2.3 fusion.28
  877.6 7.1 fusion.15
  884.7 6.9 fusion.27
  891.7 1.5 fusion.44
  (53 shorter events, 11.6 us)
Async XLA Ops:
  6.5 4.0 copy-start
  6.5 254.4 %all-gather.3.cloned.1.call-start = ((), (), s32[]{:S(2)}) async-start(), calls=%async_computation.1 | async-start | bytes 43130880 | tf_op jit(solution)/shard_map/all_gather | solution.py:19
  13.5 9.6 %copy-start.2 = (f32[162,8,8,128]{3,2,1,0:T(8,128)}, f32[162,8,8,128]{3,2,1,0:T(8,128)S(1)}, u32[]{:S(2)}) copy-start(f32[162,8,8,128]{3,2,1,0:T(8,128)S(1)} %copy.22) | copy-start | bytes 15925252
  23.1 3.1 copy-start.4
  23.1 4.3 copy-start.6
  23.1 756.7 %all-reduce.2.cloned.1.call-start = ((), (), s32[]{:S(2)}) async-start(), calls=%async_computation | async-start | bytes 1327104 | tf_op jit(solution)/shard_map/psum | solution.py:93
  26.1 86.8 %collective-permute-start = (bf16[1296,128]{1,0:T(8,128)(2,1)S(1)}, bf16[1296,128]{1,0:T(8,128)(2,1)S(1)}, u32[]{:S(2)}, u32[]{:S(2)}) collective-permute-start(bf16[1296,128]{1,0:T(8,128)(2,1)S(1)} %bitcast.73), channel_id=1, source_target_pairs={{0,2},{2,4},{4,6},{6,8},{8,10},{10,12},{12,14},{14,16},{16,18},{18... | collective-permute-start | bytes 995336 | tf_op jit(solution)/shard_map/ppermute | solution.py:14
  795.1 2.4 copy-start.3
  820.8 9.6 %copy-start.5 = (s32[6,2]{0,1:T(2,128)S(1)}, s32[6,2]{0,1:T(2,128)}, u32[]{:S(2)}) copy-start(s32[6,2]{0,1:T(2,128)} %param.21) | copy-start | bytes 148
  820.8 35.9 %copy-start.7 = (f32[648]{0:T(1024)S(1)}, f32[648]{0:T(1024)}, u32[]{:S(2)}) copy-start(f32[648]{0:T(1024)} %param.20) | copy-start | bytes 7780
  820.8 35.9 %copy-start.8 = (f32[648]{0:T(1024)S(1)}, f32[648]{0:T(1024)}, u32[]{:S(2)}) copy-start(f32[648]{0:T(1024)} %param.19) | copy-start | bytes 7780
  826.9 30.0 %collective-permute-start.1 = (bf16[1296,8,2,8]{0,3,2,1:T(8,128)(2,1)S(1)}, bf16[1296,8,2,8]{0,3,2,1:T(8,128)(2,1)S(1)}, u32[]{:S(2)}, u32[]{:S(2)}) collective-permute-start(bf16[1296,8,2,8]{0,3,2,1:T(8,128)(2,1)S(1)} %get-tuple-element.79), channel_id=1, source_target_pairs={{0,1},{1,0},{2,3},{3,2},{4,5},{5,4},{6,7},{7,6},{8,9},{9,8},{10,11... | collective-permute-start | bytes 995336 | tf_op jit(solution)/shard_map/ppermute | solution.py:36
  830.1 26.9 %collective-permute-start.2 = (bf16[1296,8,2,8]{0,3,2,1:T(8,128)(2,1)S(1)}, bf16[1296,8,2,8]{0,3,2,1:T(8,128)(2,1)S(1)}, u32[]{:S(2)}, u32[]{:S(2)}) collective-permute-start(bf16[1296,8,2,8]{0,3,2,1:T(8,128)(2,1)S(1)} %get-tuple-element.80), channel_id=1, source_target_pairs={{1,0},{0,1},{3,2},{2,3},{5,4},{4,5},{7,6},{6,7},{9,8},{8,9},{11,10... | collective-permute-start | bytes 995336 | tf_op jit(solution)/shard_map/ppermute | solution.py:39
  884.7 7.0 copy-start.9
  891.7 2.6 copy-start.1
Sparse Core Ops, SparseCore 0:
  23.2 237.6 all-gather.2
  263.4 516.2 all-reduce.1
where the time goes:
time: 905 us; the launch traced here: 901 us
  waiting for transfers between devices  666 us (74%)
  blocking collectives  85.2 us (9%)
  other arithmetic  41.8 us (5%)
  between operations  39.3 us (4%)
  local copies, waits for them, and re-layouts  38 us (4%)
  matrix products  26.5 us (3%)
    psum x1, waiting for transfers between devices, body(): lap_sum = lax.psum(scaled, 'gz')  519 us
    all_gather x1, waiting for transfers between devices, entering_2(): gathered = jax.tree.map(lambda a: lax.all_gather(a, axis), part)  148 us
    all_gather x1, blocking collectives, entering_2(): gathered = jax.tree.map(lambda a: lax.all_gather(a, axis), part)  85.2 us
    scatter-add x1, local copies, waits for them, and re-layouts, build_upward(): upward = upward.at[:, 0, :].add(-factor * before_term)  18.9 us
  transfers between devices with their start and end apart: 5, of which 2 were waited for; matrix products, arithmetic and copies ran while one was open for 1% of the time, Pallas kernels for 0%

commit v1 on v0

--- a/solution.py
+++ b/solution.py
@@ -90,7 +90,7 @@
     identity = (jnp.ones_like(slab_decay), jnp.zeros_like(outgoing))
     _, prefix = entering_2((slab_decay, outgoing), "gz", combine, identity)
     scaled = jnp.exp(-rate_col * (layers * (loop_size - 1.0 - slab_pos))) * outgoing
-    lap_sum = lax.psum(scaled, "gz")
+    lap_sum = jnp.sum(lax.all_gather(scaled, "gz"), axis=0)
     entering = prefix + jnp.exp(-rate_col * (layers * slab_pos)) * lap_sum / lap_gain
     upward = build_upward(box_terms, entering, before_term, rate_col, factor)
     field_grid = upward.astype(jnp.bfloat16).reshape(exp_rows, layers, columns, BY)

time: 905 us -> 710 us (0.78)
  the two profiles are of different devices: /device:TPU:0 before, /device:TPU:111 now
where the time goes in v1:
time: 710 us; the launch traced here: 706 us
  waiting for transfers between devices  375 us (53%)
  other arithmetic  143 us (20%)
  blocking collectives  77.7 us (11%)
  local copies, waits for them, and re-layouts  39.6 us (6%)
  between operations  39.3 us (6%)
  matrix products  25.7 us (4%)
    all_gather x1, waiting for transfers between devices, entering_2(): gathered = jax.tree.map(lambda a: lax.all_gather(a, axis), part)  220 us
    all_gather x1, waiting for transfers between devices, body(): lap_sum = jnp.sum(lax.all_gather(scaled, 'gz'), axis=0)  154 us
    add x63, other arithmetic, combine(): return (earlier[0] * later[0], later[0] * earlier[1] + later[1])  86.8 us
    all_gather x1, blocking collectives, entering_2(): gathered = jax.tree.map(lambda a: lax.all_gather(a, axis), part)  77.7 us
    scatter-add x1, local copies, waits for them, and re-layouts, build_upward(): upward = upward.at[:, 0, :].add(-factor * before_term)  18.9 us
    reduce_sum x1, other arithmetic, body(): lap_sum = jnp.sum(lax.all_gather(scaled, 'gz'), axis=0)  15.7 us
    concatenate x6, other arithmetic, body(): moved = jnp.roll(moved, step_y, axis=3)  15.2 us
  transfers between devices with their start and end apart: 5, of which 2 were waited for; matrix products, arithmetic and copies ran while one was open for 3% of the time, Pallas kernels for 0%

profile of v1, /device:TPU:111, one launch (start us, length us, event | category | flops | bytes accessed | tf_op | source)
XLA Modules:
  0.0 706.3 jit_solution(16840397034992762555)
XLA Ops:
  10.6 1.6 multiply_bitcast_fusion
  13.5 8.9 %fusion.68 = f32[1296,1,128]{2,1,0:T(1,128)S(1)} fusion(f32[1296,8,1]{1,2,0:T(1,128)S(1)} %copy.17, f32[1296,8,128]{2,1,0:T(8,128)S(1)} %bitcast.61), kind=kOutput, calls=%fused_computation.135 | convolution fusion | flops 15925248 | bytes 6013440 | tf_op jit(solution)/shard_map/kz,kzb->kb/dot_general | solution.py:80
  24.2 2.9 slice.133
  27.6 77.7 %all_gather.16 = f32[64,1296,1]{1,2,0:T(1,128)S(1)} all-gather(f32[1,1296,1]{1,2,0:T(1,128)S(1)} %fusion.49), channel_id=1, replica_groups=mesh['gz'=64,'xy'=2] {'gz'}, dimensions={0}, use_global_device_ids=true | all-gather | bytes 336960 | tf_op jit(solution)/shard_map/all_gather | solution.py:19
  105.5 154.3 %all-gather.7.cloned.1.call-done = f32[82944,128]{1,0:T(8,128)} async-done(((f32[1296,128]{1,0:T(8,128)}), f32[82944,128]{1,0:T(8,128)}) %all-gather.7.cloned.1.call-update) | async-done | bytes 42467344 | tf_op jit(solution)/shard_map/all_gather | solution.py:93
  259.8 15.7 %reduce_sum.9 = f32[1296,128]{1,0:T(8,128)S(1)} reduce(f32[64,1296,128]{2,1,0:T(8,128)} %bitcast.60, f32[]{:T(128)} %constant.95.clone.1), dimensions={0}, to_apply=%region_2.3 | reduce | flops 10450944 | bytes 43130884 | tf_op jit(solution)/shard_map/reduce_sum | solution.py:93
  275.5 220.0 %all-gather.5.cloned.1.call-done = f32[82944,128]{1,0:T(8,128)} async-done(((f32[1296,128]{1,0:T(8,128)}), f32[82944,128]{1,0:T(8,128)}) %all-gather.5.cloned.1.call-update) | async-done | bytes 42467344 | tf_op jit(solution)/shard_map/all_gather | solution.py:19
  495.6 91.1 %while.13 = (s32[]{:T(128)}, f32[1296,128]{1,0:T(8,128)S(1)}, s32[]{:T(128)}, f32[64,1296,1]{1,2,0:T(1,128)S(1)}, f32[64,1296,128]{2,1,0:T(8,128)}, /*index=5*/s32[]{:T(128)}, s32[]{:T(128)}, s32[]{:T(128)}) while((s32[]{:T(128)}, f32[1296,128]{1,0:T(8,128)S(1)}, s32[]{:T(128)}, f32[64,1296,1]{1,2,0:T(1,128)S(1)}, f32[64,1296,128]{2,1,0:T(8,128)}, ...), condition=%wide.region_1.2_spmd, body=%wide.region_0.1_spmd.sunk | while | flops 331781 | bytes 2006335 | solution.py:27
  587.1 13.8 %multiply_add_fusion = f32[1296,8,128]{2,1,0:T(8,128)S(1)} fusion(f32[1296,128]{1,0:T(8,128)S(1)} %divide_add_fusion, f32[1296,8]{1,0:T(8,128)S(1)} %copy.14, f32[1296,8,128]{2,1,0:T(8,128)} %bitcast.63, f32[8,8]{1,0:T(8,128)S(1)} %fusion.50, f32[1296]{0:T(1024)S(1)} %get-tuple-element.100, pred[8,8]{1,0:T(8,128)(4,1)S(1)} %fusion.51), kind=kOutput, calls=%fused_computation.14 | convolution fusion | flops 130222080 | bytes 11327360 | tf_op jit(solution)/shard_map/kij,kjb->kib/dot_general | solution.py:53
  600.9 2.4 copy-done.3
  603.9 18.9 %scatter-add.4 = f32[1296,8,128]{2,1,0:T(8,128)} dynamic-update-slice(f32[1296,8,128]{2,1,0:T(8,128)} %copy-done.3, f32[1296,1,128]{2,1,0:T(1,128)S(1)} %slice_add_fusion, s32[]{:T(128)} %constant.97.clone.1, s32[]{:T(128)} %constant.97.clone.1, s32[]{:T(128)} %constant.97.clone.1) | dynamic-update-slice | bytes 1327108 | tf_op jit(solution)/shard_map/scatter-add | solution.py:57
  622.8 3.8 convert_element_type.126
  626.6 4.9 copy.16
  632.6 1.9 collective-permute-start.1
  662.1 2.1 pad_maximum_fusion
  664.2 3.4 constant_dynamic-slice_fusion.5
  667.6 4.7 fusion.29
  672.3 2.0 fusion.30
  674.3 2.0 fusion.31
  676.4 2.1 fusion.32
  678.4 2.1 fusion.33
  680.5 2.3 fusion.28
  682.8 7.1 %fusion.15 = bf16[648,8,16,8]{0,3,2,1:T(8,128)(2,1)S(1)} fusion(f32[648]{0:T(1024)S(1)} %get-tuple-element.84, f32[648]{0:T(1024)S(1)} %get-tuple-element.93, f32[648]{0:T(1024)S(1)} %get-tuple-element.85, f32[648]{0:T(1024)S(1)} %get-tuple-element.94, f32[648]{0:T(1024)S(1)} %get-tuple-element.86, f32[648]{0:T(1024)S(1)} %get-tuple-element.90, ...), kind=kLoop, calls=%fused_computation.56 | loop fusion | flops 23887872 | bytes 17283456 | tf_op jit(solution)/shard_map/convert.3
  689.9 6.9 fusion.27
  (180 shorter events, 103.1 us)
Async XLA Ops:
  6.5 4.0 copy-start
  6.5 253.3 %all-gather.7.cloned.1.call-start = ((), (), s32[]{:S(2)}) async-start(), calls=%async_computation.1 | async-start | bytes 43130880 | tf_op jit(solution)/shard_map/all_gather | solution.py:93
  13.5 8.9 %copy-start.2 = (f32[162,8,8,128]{3,2,1,0:T(8,128)}, f32[162,8,8,128]{3,2,1,0:T(8,128)S(1)}, u32[]{:S(2)}) copy-start(f32[162,8,8,128]{3,2,1,0:T(8,128)S(1)} %copy.22) | copy-start | bytes 15925252
  22.3 1.2 copy-start.4
  22.4 4.9 copy-start.6
  23.5 472.1 %all-gather.5.cloned.1.call-start = ((), (), s32[]{:S(2)}) async-start(), calls=%async_computation | async-start | bytes 43130880 | tf_op jit(solution)/shard_map/all_gather | solution.py:19
  27.2 78.1 %collective-permute-start = (bf16[1296,128]{1,0:T(8,128)(2,1)S(1)}, bf16[1296,128]{1,0:T(8,128)(2,1)S(1)}, u32[]{:S(2)}, u32[]{:S(2)}) collective-permute-start(bf16[1296,128]{1,0:T(8,128)(2,1)S(1)} %bitcast.75), channel_id=1, source_target_pairs={{0,2},{2,4},{4,6},{6,8},{8,10},{10,12},{12,14},{14,16},{16,18},{18... | collective-permute-start | bytes 995336 | tf_op jit(solution)/shard_map/ppermute | solution.py:14
  600.9 2.4 copy-start.3
  626.6 9.1 %copy-start.5 = (s32[6,2]{0,1:T(2,128)S(1)}, s32[6,2]{0,1:T(2,128)}, u32[]{:S(2)}) copy-start(s32[6,2]{0,1:T(2,128)} %param.21) | copy-start | bytes 148
  626.6 35.4 %copy-start.7 = (f32[648]{0:T(1024)S(1)}, f32[648]{0:T(1024)}, u32[]{:S(2)}) copy-start(f32[648]{0:T(1024)} %param.20) | copy-start | bytes 7780
  626.6 35.4 %copy-start.8 = (f32[648]{0:T(1024)S(1)}, f32[648]{0:T(1024)}, u32[]{:S(2)}) copy-start(f32[648]{0:T(1024)} %param.19) | copy-start | bytes 7780
  632.6 29.5 %collective-permute-start.1 = (bf16[1296,8,2,8]{0,3,2,1:T(8,128)(2,1)S(1)}, bf16[1296,8,2,8]{0,3,2,1:T(8,128)(2,1)S(1)}, u32[]{:S(2)}, u32[]{:S(2)}) collective-permute-start(bf16[1296,8,2,8]{0,3,2,1:T(8,128)(2,1)S(1)} %get-tuple-element.79), channel_id=1, source_target_pairs={{0,1},{1,0},{2,3},{3,2},{4,5},{5,4},{6,7},{7,6},{8,9},{9,8},{10,11... | collective-permute-start | bytes 995336 | tf_op jit(solution)/shard_map/ppermute | solution.py:36
  634.5 27.6 %collective-permute-start.2 = (bf16[1296,8,2,8]{0,3,2,1:T(8,128)(2,1)S(1)}, bf16[1296,8,2,8]{0,3,2,1:T(8,128)(2,1)S(1)}, u32[]{:S(2)}, u32[]{:S(2)}) collective-permute-start(bf16[1296,8,2,8]{0,3,2,1:T(8,128)(2,1)S(1)} %get-tuple-element.80), channel_id=1, source_target_pairs={{1,0},{0,1},{3,2},{2,3},{5,4},{4,5},{7,6},{6,7},{9,8},{8,9},{11,10... | collective-permute-start | bytes 995336 | tf_op jit(solution)/shard_map/ppermute | solution.py:39
  689.9 7.0 copy-start.9
  696.8 2.6 copy-start.1
Sparse Core Ops, SparseCore 0:
  23.6 236.1 all-gather.6
  261.6 233.9 all-gather.4
